TPU v7x, 256 devices: a whole 4x4x8 slice. The times are simulated.
256 devices in a mesh: chan: 8 (over z_hi, x), tm: 16 (over z_lo, y), dp: 2 (over core).
Axes of the slice: x: 4, y: 4, z: 8 (z_hi: 2, z_lo: 4; z = z_hi * 4 + z_lo), core: 2. Of those that a mesh axis runs over, the one named last changes fastest.
Arguments:
- contexts: bfloat16 [512, 4, 16384], P('tm', 'dp', 'chan'), may hold values from -6 to 6
- cotangent: bfloat16 [512, 4, 16384], P('tm', 'dp', 'chan'), may hold values from -6 to 6
- w_in: bfloat16 [16384, 8192], P('chan', 'tm'), may hold values from -0.046875 to 0.046875
- w_out: bfloat16 [8192, 16384], P('tm', 'chan'), may hold values from -0.0625 to 0.0625
- time_weight: bfloat16 [512, 512], replicated, may hold values from -0.25 to 0.25
Outputs:
- grad_contexts: bfloat16 [512, 4, 16384], P('tm', 'dp', 'chan')
- grad_w_in: float32 [16384, 8192], P('chan', ('tm', 'dp'))
- grad_w_out: float32 [8192, 16384], P(('tm', 'dp'), 'chan')
- grad_time: float32 [512, 512], replicated
All inputs are finite; a program needn't handle non-finite values.
Results may differ from a plain program's by a relative error of at most 0.0057.
Values may be sent and summed in bfloat16 or wider, within the bound.
No kernel may reach another device: no remote copies, remote signals or barrier semaphores. Data moves between devices by JAX's collectives and lax.ppermute only.
A program may use at most 192 MiB of HBM per device.

v0:
```python
import functools
import math
import jax
import jax.numpy as jnp
from jax import lax
from jax.sharding import Mesh
from jax.sharding import PartitionSpec as P

TM = ("tz", "ty")
CHAN = ("zh", "cx")
tanh_scale = math.sqrt(2.0 / math.pi)
cubic_term = 0.044715


def gelu_pair(value):
    inner = jnp.tanh(tanh_scale * (value + cubic_term * value * value * value))
    result = 0.5 * value * (1.0 + inner)
    slope = 0.5 * (1.0 + inner) + 0.5 * value * (1.0 - inner * inner) * tanh_scale * (
        1.0 + 3.0 * cubic_term * value * value
    )
    return (result, slope)


def hidden_finish(hidden_pre, hidden_grad):
    act_hidden, slope_hidden = gelu_pair(hidden_pre)
    return (act_hidden.astype(jnp.bfloat16), (hidden_grad * slope_hidden).astype(jnp.bfloat16))


def gather_a2a(x, axis_name, size):
    b = jnp.broadcast_to(x[None], (size,) + x.shape)
    y = lax.all_to_all(b, axis_name, 0, 0, tiled=True)
    return y.reshape((size * x.shape[0],) + x.shape[1:])


def scatter_a2a(p, axis_name, size):
    y = lax.all_to_all(
        p.reshape((size, p.shape[0] // size) + p.shape[1:]), axis_name, 0, 0, tiled=True
    )
    return y.sum(0)


def on_device(contexts, cotangent, w_in, w_out, time_weight, tm, chan, chan_near, stages):
    local_len, batch_dev, width_dev = contexts.shape
    own = jnp.stack([contexts, cotangent]).transpose(0, 2, 1, 3)
    pair = lax.all_gather(own, TM, axis=2, tiled=True)
    whole_x, whole_dy = (pair[0], pair[1])
    length = whole_x.shape[1]
    pre_time = jnp.einsum("tl,blc->btc", time_weight, whole_x, preferred_element_type=jnp.float32)
    act_time, slope_time = gelu_pair(pre_time)
    mixed = (whole_x.astype(jnp.float32) + act_time).astype(jnp.bfloat16)
    rows = batch_dev * length
    mixed_rows = mixed.reshape(rows, width_dev)
    grad_rows = whole_dy.reshape(rows, width_dev)
    hidden_part = jnp.dot(mixed_rows, w_in, preferred_element_type=jnp.float32)
    hgrad_part = jnp.einsum("rc,hc->rh", grad_rows, w_out, preferred_element_type=jnp.float32)
    summed = scatter_a2a(jnp.stack([hidden_part, hgrad_part], 1), "cx", chan_near)
    summed = scatter_a2a(summed, "zh", chan // chan_near)
    act_rows, pre_grad_rows = hidden_finish(summed[:, 0], summed[:, 1])
    fin = gather_a2a(jnp.stack([act_rows, pre_grad_rows], 1), "zh", chan // chan_near)
    fin = gather_a2a(fin, "cx", chan_near)
    activation, pre_grad = (fin[:, 0], fin[:, 1])
    win_part = jnp.einsum("rc,rh->ch", mixed_rows, pre_grad, preferred_element_type=jnp.float32)
    wout_part = jnp.einsum("rh,rc->hc", activation, grad_rows, preferred_element_type=jnp.float32)
    grad_w_in, grad_w_out = (
        lax.psum_scatter(win_part, "dp", scatter_dimension=1, tiled=True),
        lax.psum_scatter(wout_part, "dp", scatter_dimension=0, tiled=True),
    )
    share = jnp.einsum(
        "rh,ch->rc", pre_grad, w_in, preferred_element_type=jnp.float32
    ) + grad_rows.astype(jnp.float32) * (1.0 / tm)
    share = share.reshape(batch_dev, length, width_dev)
    gate = (share * slope_time).astype(jnp.bfloat16)
    back = jnp.einsum("tl,btc->blc", time_weight, gate, preferred_element_type=jnp.float32)
    grad_own = lax.psum_scatter(share + back, TM, scatter_dimension=1, tiled=True)
    grad_contexts = grad_own.astype(jnp.bfloat16).transpose(1, 0, 2)
    time_part = jnp.einsum("btc,blc->tl", gate, whole_x, preferred_element_type=jnp.float32)
    for names, size in stages:
        time_part = scatter_a2a(time_part, names, size)
    for names, size in stages[::-1]:
        time_part = gather_a2a(time_part, names, size)
    grad_time = time_part
    return (grad_contexts, grad_w_in, grad_w_out, grad_time)


def solution(mesh):
    chan, tm, dp = (mesh.shape["chan"], mesh.shape["tm"], mesh.shape["dp"])
    far, near_z = (2, 4)
    fine = Mesh(
        mesh.devices.reshape(far, chan // far, near_z, tm // near_z, dp),
        ("zh", "cx", "tz", "ty", "dp"),
    )
    step = functools.partial(
        on_device,
        tm=tm,
        chan=chan,
        chan_near=chan // far,
        stages=((("dp",), dp), (("cx",), chan // far), (("zh",), far), (TM, tm)),
    )
    token = P(TM, "dp", CHAN)
    return jax.shard_map(
        step,
        mesh=fine,
        in_specs=(token, token, P(CHAN, TM), P(TM, CHAN), P()),
        out_specs=(token, P(CHAN, TM + ("dp",)), P(TM + ("dp",), CHAN), P()),
        check_vma=False,
    )
```

profile of v0, /device:TPU:1, one launch (start us, length us, event | category | flops | bytes accessed | tf_op | source)
XLA Modules:
  0.0 436.8 jit_solution(6076313547695591283)
XLA Ops:
  7.2 0.0 copy-start
  7.2 0.0 all-gather.2.cloned.1.call-start
  7.2 1.3 copy_bitcast_fusion
  8.6 0.8 maximum_bitcast_fusion
  9.4 0.0 all-gather.2.cloned.1.call-update
  9.4 0.0 reduce-scatter.4.cloned.1.call-start
  9.5 107.0 %all-gather.2.cloned.1.call-done = bf16[2,2,512,2048]{3,2,1,0:T(8,128)(2,1)} async-done(((bf16[2,2,32,2048]{3,2,1,0:T(8,128)(2,1)}), bf16[2,2,512,2048]{3,2,1,0:T(8,128)(2,1)}) %all-gather.2.cloned.1.call-update) | async-done | bytes 8388624 | tf_op jit(solution)/shard_map/all_gather | solution.py:45
  116.4 2.7 slice.25
  119.1 0.0 copy-start.2
  119.1 0.2 copy-done.9
  119.3 2.4 fusion.20
  121.7 0.0 copy-done.2
  121.7 0.0 slice-done.2
  121.7 1.7 slice-done.3
  123.5 6.5 %add_convert_fusion = (bf16[2,512,2048]{2,1,0:T(8,128)(2,1)S(1)}, f32[2,2048,512]{1,2,0:T(8,128)}) fusion(bf16[2,2,512,2048]{3,2,1,0:T(8,128)(2,1)S(1)} %bitcast.104, bf16[512,512]{1,0:T(8,128)(2,1)S(1)} %copy-done.7), kind=kOutput, calls=%fused_computation.12 | convolution fusion | flops 2170552320 | bytes 21495808 | tf_op jit(solution)/shard_map/tl,blc->btc/dot_general | solution.py:48
  130.0 0.0 copy-done
  130.0 2.3 fusion.17
  132.3 0.4 pad_maximum_fusion
  132.8 0.4 copy.61
  133.2 51.6 %all_to_all.60 = f32[4,256,2,512]{3,1,2,0:T(8,128)} all-to-all(f32[4,256,2,512]{3,1,2,0:T(8,128)S(1)} %copy.61), channel_id=1, replica_groups=mesh['zh'=2,'cx'=4,'tz'=4,'ty'=4,'dp'=2] {'cx'}, dimensions={0} | all-to-all | bytes 8388608 | tf_op jit(solution)/shard_map/all_to_all | solution.py:36
  184.9 2.8 reduce_sum.54
  187.6 0.1 copy.63
  187.7 21.7 %all_to_all.61 = f32[2,128,2,512]{3,1,2,0:T(8,128)S(1)} all-to-all(f32[2,128,2,512]{3,1,2,0:T(8,128)S(1)} %copy.63), channel_id=1, replica_groups=mesh['zh'=2,'cx'=4,'tz'=4,'ty'=4,'dp'=2] {'zh'}, dimensions={0} | all-to-all | bytes 2097152 | tf_op jit(solution)/shard_map/all_to_all | solution.py:36
  209.5 0.9 reduce_sum.55
  210.4 1.2 multiply_convert_fusion
  211.7 11.7 %all_to_all.62 = bf16[2,128,2,512]{3,1,2,0:T(8,128)(2,1)S(1)} all-to-all(bf16[2,128,2,512]{3,1,2,0:T(8,128)(2,1)S(1)} %broadcast_in_dim.40), channel_id=1, replica_groups=mesh['zh'=2,'cx'=4,'tz'=4,'ty'=4,'dp'=2] {'zh'}, dimensions={0} | all-to-all | bytes 1048576 | tf_op jit(solution)/shard_map/all_to_all | solution.py:31
  223.4 0.2 broadcast_in_dim.42
  223.6 0.0 copy-start.3
  223.6 18.1 %all_to_all.63 = bf16[4,256,2,512]{3,1,2,0:T(8,128)(2,1)S(1)} all-to-all(bf16[4,256,2,512]{3,1,2,0:T(8,128)(2,1)S(1)} %broadcast_in_dim.42), channel_id=1, replica_groups=mesh['zh'=2,'cx'=4,'tz'=4,'ty'=4,'dp'=2] {'cx'}, dimensions={0} | all-to-all | bytes 4194304 | tf_op jit(solution)/shard_map/all_to_all | solution.py:31
  241.7 0.1 copy.65
  241.9 0.0 copy-start.5
  241.9 0.0 slice-start
  241.9 0.0 copy-done.3
  241.9 0.0 slice-start.1
  241.9 2.4 multiply_add_fusion.1
  244.3 0.5 slice-done
  244.8 1.3 slice-done.1
  246.1 5.5 %fusion.6 = bf16[2,512,2048]{2,1,0:T(8,128)(2,1)S(1)} fusion(f32[2,512,2048]{2,1,0:T(8,128)S(1)} %bitcast.88, f32[2,2048,512]{1,2,0:T(8,128)S(1)} %bitcast.95), kind=kLoop, calls=%fused_computation.8 | loop fusion | flops 39845888 | bytes 20971520 | tf_op jit(solution)/shard_map/convert_element_type | solution.py:72
  251.6 0.0 copy-start.4
  251.6 1.9 copy-done.4
  253.5 6.0 %bitcast_add_fusion = f32[2,512,2048]{2,1,0:T(8,128)} fusion(f32[2,512,2048]{2,1,0:T(8,128)S(1)} %bitcast.89, bf16[2,512,2048]{2,1,0:T(8,128)(2,1)S(1)} %fusion.6, bf16[512,512]{1,0:T(8,128)(2,1)S(1)} %copy-done.8), kind=kOutput, calls=%fused_computation.9 | convolution fusion | flops 2149580800 | bytes 21495808 | tf_op jit(solution)/shard_map/tl,btc->blc/dot_general | solution.py:73
  259.5 0.0 reduce-scatter.4.cloned.1.call-update
  259.5 0.0 reduce-scatter.6.cloned.1.call-start
  259.5 1.5 copy-done.6
  261.1 6.5 %fusion.27 = f32[2048,512]{1,0:T(8,128)} fusion(bf16[1024,2048]{1,0:T(8,128)(2,1)} %bitcast.109, bf16[1024,2,512]{2,0,1:T(8,128)(2,1)S(1)} %bitcast.97), kind=kOutput, calls=%fused_computation.30 | convolution fusion | flops 2147483648 | bytes 9437184 | tf_op jit(solution)/shard_map/rc,rh->ch/dot_general | solution.py:62
  267.6 0.0 reduce-scatter.6.cloned.1.call-update
  267.6 0.3 reduce-scatter.8.cloned.1.call-start
  267.9 6.5 %fusion.26 = f32[512,2048]{1,0:T(8,128)} fusion(bf16[1024,2048]{1,0:T(8,128)(2,1)} %bitcast.91, bf16[1024,2,512]{2,0,1:T(8,128)(2,1)S(1)} %bitcast.98), kind=kOutput, calls=%fused_computation.28 | convolution fusion | flops 2147483648 | bytes 9437184 | tf_op jit(solution)/shard_map/rh,rc->hc/dot_general | solution.py:63
  274.4 0.0 reduce-scatter.8.cloned.1.call-update
  274.5 5.8 %fusion.23 = f32[2,256,512]{2,1,0:T(8,128)S(1)} fusion(bf16[2,256,2,2048]{3,1,0,2:T(8,128)(2,1)} %bitcast.93, bf16[2,2,512,2048]{3,2,1,0:T(8,128)(2,1)} %all-gather.2.cloned.1.call-done), kind=kOutput, calls=%fused_computation.26 | convolution fusion | flops 2147483648 | bytes 9437184 | tf_op jit(solution)/shard_map/btc,blc->tl/dot_general | solution.py:76
  280.3 20.9 %all_to_all.64 = f32[2,256,512]{2,1,0:T(8,128)S(1)} all-to-all(f32[2,256,512]{2,1,0:T(8,128)S(1)} %fusion.23), channel_id=1, replica_groups=mesh['zh'=2,'cx'=4,'tz'=4,'ty'=4,'dp'=2] {'dp'}, dimensions={0} | all-to-all | bytes 2097152 | tf_op jit(solution)/shard_map/all_to_all | solution.py:36
  301.2 0.1 reduce_sum.56
  301.3 11.5 %all_to_all.65 = f32[4,64,512]{2,1,0:T(8,128)S(1)} all-to-all(f32[4,64,512]{2,1,0:T(8,128)S(1)} %bitcast.105), channel_id=1, replica_groups=mesh['zh'=2,'cx'=4,'tz'=4,'ty'=4,'dp'=2] {'cx'}, dimensions={0} | all-to-all | bytes 1048576 | tf_op jit(solution)/shard_map/all_to_all | solution.py:36
  312.8 11.3 %all_to_all.66 = f32[2,32,512]{2,1,0:T(8,128)S(1)} all-to-all(f32[2,32,512]{2,1,0:T(8,128)S(1)} %bitcast.107), channel_id=1, replica_groups=mesh['zh'=2,'cx'=4,'tz'=4,'ty'=4,'dp'=2] {'zh'}, dimensions={0} | all-to-all | bytes 262144 | tf_op jit(solution)/shard_map/all_to_all | solution.py:36
  324.2 43.5 %all_to_all.67 = f32[16,2,512]{2,1,0:T(2,128)S(1)} all-to-all(f32[16,2,512]{2,1,0:T(2,128)S(1)} %reshape.63), channel_id=1, replica_groups=mesh['zh'=2,'cx'=4,'tz'=4,'ty'=4,'dp'=2] {'tz','ty'}, dimensions={0} | all-to-all | bytes 131072 | tf_op jit(solution)/shard_map/all_to_all | solution.py:36
  367.8 26.0 %all_to_all.68 = f32[16,2,512]{2,1,0:T(2,128)S(1)} all-to-all(f32[16,2,512]{2,1,0:T(2,128)S(1)} %broadcast_in_dim.43), channel_id=1, replica_groups=mesh['zh'=2,'cx'=4,'tz'=4,'ty'=4,'dp'=2] {'tz','ty'}, dimensions={0} | all-to-all | bytes 131072 | tf_op jit(solution)/shard_map/all_to_all | solution.py:31
  393.8 11.3 %all_to_all.69 = f32[2,32,512]{2,1,0:T(8,128)S(1)} all-to-all(f32[2,32,512]{2,1,0:T(8,128)S(1)} %broadcast_in_dim.45), channel_id=1, replica_groups=mesh['zh'=2,'cx'=4,'tz'=4,'ty'=4,'dp'=2] {'zh'}, dimensions={0} | all-to-all | bytes 262144 | tf_op jit(solution)/shard_map/all_to_all | solution.py:31
  405.2 10.5 %all_to_all.70 = f32[4,64,512]{2,1,0:T(8,128)S(1)} all-to-all(f32[4,64,512]{2,1,0:T(8,128)S(1)} %broadcast_in_dim.47), channel_id=1, replica_groups=mesh['zh'=2,'cx'=4,'tz'=4,'ty'=4,'dp'=2] {'cx'}, dimensions={0} | all-to-all | bytes 1048576 | tf_op jit(solution)/shard_map/all_to_all | solution.py:31
  415.8 0.1 broadcast_in_dim.49
  415.9 9.2 %all_to_all.71 = f32[2,256,512]{2,1,0:T(8,128)S(1)} all-to-all(f32[2,256,512]{2,1,0:T(8,128)S(1)} %broadcast_in_dim.49), channel_id=1, replica_groups=mesh['zh'=2,'cx'=4,'tz'=4,'ty'=4,'dp'=2] {'dp'}, dimensions={0} | all-to-all | bytes 2097152 | tf_op jit(solution)/shard_map/all_to_all | solution.py:31
  425.1 1.2 convert_bitcast_fusion
  426.3 1.0 copy.69
  427.3 2.0 reduce-scatter.8.cloned.1.call-done
  429.3 1.0 copy.78
  (28 shorter events, 0.4 us)
Async XLA Ops:
  7.2 122.8 %copy-start = (bf16[2048,512]{1,0:T(8,128)(2,1)S(1)}, bf16[2048,512]{1,0:T(8,128)(2,1)}, u32[]{:S(2)}) copy-start(bf16[2048,512]{1,0:T(8,128)(2,1)} %param.7) | copy-start | bytes 6291460
  7.2 109.3 %all-gather.2.cloned.1.call-start = ((), (), s32[]{:S(2)}) async-start(), calls=%async_computation.15 | async-start | bytes 8912896 | tf_op jit(solution)/shard_map/all_gather | solution.py:45
  9.4 415.7 %reduce-scatter.4.cloned.1.call-start = ((), (), s32[]{:S(2)}) async-start(), calls=%async_computation.16 | async-start | bytes 8912896 | tf_op jit(solution)/shard_map/reduce_scatter | solution.py:74
  116.4 2.9 copy-start.9
  116.4 5.3 %slice-start.2 = ((s8[8388608]{0:T(1024)(128)(4,1)}), s8[4194304]{0:T(1024)(128)(4,1)S(1)}, s32[]{:S(2)}) async-start(s8[8388608]{0:T(1024)(128)(4,1)} %bitcast.103), calls=%async_computation.21 | async-start | bytes 8388608
  119.1 2.6 copy-start.2
  119.3 4.2 slice-start.3
  119.3 4.2 copy-start.7
  130.0 2.3 copy-start.10
  223.6 18.3 %copy-start.3 = (bf16[1,2,512,2048]{3,2,1,0:T(8,128)(2,1)S(1)}, bf16[1,2,512,2048]{3,2,1,0:T(8,128)(2,1)}, u32[]{:S(2)}) copy-start(bf16[1,2,512,2048]{3,2,1,0:T(8,128)(2,1)} %copy-done.2) | copy-start | bytes 12582916
  241.9 2.5 copy-start.5
  241.9 2.9 slice-start
  241.9 4.2 slice-start.1
  246.1 7.4 %copy-start.8 = (bf16[512,512]{1,0:T(8,128)(2,1)S(1)}, bf16[512,512]{1,0:T(8,128)(2,1)}, u32[]{:S(2)}) copy-start(bf16[512,512]{1,0:T(8,128)(2,1)} %param.9) | copy-start | bytes 1572868
  251.6 1.9 copy-start.4
  259.5 1.6 copy-start.6
  259.5 167.8 %reduce-scatter.6.cloned.1.call-start = ((), (), s32[]{:S(2)}) async-start(), calls=%async_computation.17 | async-start | bytes 6291456 | tf_op jit(solution)/shard_map/reduce_scatter | solution.py:65
  267.6 161.7 %reduce-scatter.8.cloned.1.call-start = ((), (), s32[]{:S(2)}) async-start(), calls=%async_computation.18 | async-start | bytes 6291456 | tf_op jit(solution)/shard_map/reduce_scatter | solution.py:66
  405.2 25.1 %copy-start.1 = (bf16[2048,512]{1,0:T(8,128)(2,1)S(1)}, bf16[2048,512]{1,0:T(8,128)(2,1)}, u32[]{:S(2)}) copy-start(bf16[2048,512]{1,0:T(8,128)(2,1)} %param.7) | copy-start | bytes 6291460
Sparse Core Ops, SparseCore 0:
  10.4 106.0 all-gather.1
  259.6 123.1 reduce-scatter.3
  385.9 21.5 reduce-scatter.5
  410.4 18.7 reduce-scatter.7
where the time goes:
time: 438 us; the launch traced here: 437 us
  blocking collectives  247 us (56%)
  waiting for transfers between devices  109 us (25%)
  matrix products  38.5 us (9%)
  local copies, waits for them, and re-layouts  14.3 us (3%)
  between operations  14 us (3%)
  other arithmetic  13.1 us (3%)
    all_to_all x6, blocking collectives, scatter_a2a(): lax.all_to_all(p.reshape((size, p.shape[0] // size) + p.shape[1:]), axis_...  161 us
    all_gather x1, waiting for transfers between devices, on_device(): pair = lax.all_gather(own, TM, axis=2, tiled=True)  107 us
    all_to_all x6, blocking collectives, gather_a2a(): y = lax.all_to_all(b, axis_name, 0, 0, tiled=True)  86.8 us
    unnamed x32, local copies, waits for them, and re-layouts  9.14 us
  transfers between devices with their start and end apart: 4, of which 2 were waited for; matrix products, arithmetic and copies ran while one was open for 5% of the time, Pallas kernels for 0%

commit v1 on v0

--- a/solution.py
+++ b/solution.py
@@ -42,7 +42,12 @@
 def on_device(contexts, cotangent, w_in, w_out, time_weight, tm, chan, chan_near, stages):
     local_len, batch_dev, width_dev = contexts.shape
     own = jnp.stack([contexts, cotangent]).transpose(0, 2, 1, 3)
-    pair = lax.all_gather(own, TM, axis=2, tiled=True)
+    pair = jnp.concatenate(
+        lax.all_to_all(
+            jnp.stack(lax.axis_size(TM) * [own]), axis_name=TM, split_axis=0, concat_axis=0
+        ),
+        axis=2,
+    )
     whole_x, whole_dy = (pair[0], pair[1])
     length = whole_x.shape[1]
     pre_time = jnp.einsum("tl,blc->btc", time_weight, whole_x, preferred_element_type=jnp.float32)

time: 438 us -> 524 us (1.20)
  blocking collectives: 247 us -> 440 us
  waiting for transfers between devices: 109 us -> 2.54 us
    all_to_all x0 -> x1, blocking collectives: none -> 191 us  [on_device(): lax.all_to_all(jnp.stack(lax.axis_size(TM) * [own]), axis_name=TM, split_...]
    all_gather x1 -> x0, waiting for transfers between devices: 107 us -> none  [on_device(): pair = lax.all_gather(own, TM, axis=2, tiled=True)]
  transfers between devices with their start and end apart: 4 -> 3, of which waited for: 2 -> 1; matrix products, arithmetic and copies ran while one was open for 5% -> 4% of each run, Pallas kernels for 0% -> 0%
where the time goes in v1:
time: 524 us
  blocking collectives  440 us (84%)
  matrix products  38.5 us (7%)
  local copies, waits for them, and re-layouts  14.4 us (3%)
  other arithmetic  14.1 us (3%)
  between operations  14.1 us (3%)
    all_to_all x1, blocking collectives, on_device(): lax.all_to_all(jnp.stack(lax.axis_size(TM) * [own]), axis_name=TM, split_...  191 us
    all_to_all x6, blocking collectives, scatter_a2a(): lax.all_to_all(p.reshape((size, p.shape[0] // size) + p.shape[1:]), axis_...  157 us
    all_to_all x6, blocking collectives, gather_a2a(): y = lax.all_to_all(b, axis_name, 0, 0, tiled=True)  91.4 us
  transfers between devices with their start and end apart: 3, of which 1 were waited for; matrix products, arithmetic and copies ran while one was open for 4% of the time, Pallas kernels for 0%

profile of v1, /device:TPU:1, one launch (start us, length us, event | category | flops | bytes accessed | tf_op | source)
XLA Modules:
  0.0 523.7 jit_solution(6539046584726120981)
XLA Ops:
  7.2 0.0 copy-start
  7.2 0.0 reduce-scatter.4.cloned.1.call-start
  7.2 2.0 maximum_bitcast_fusion
  9.2 0.2 copy.65
  9.3 1.1 stack.15
  10.4 191.2 %all_to_all.65 = bf16[16,2,2,32,2048]{4,3,2,1,0:T(8,128)(2,1)S(1)} all-to-all(bf16[16,2,2,32,2048]{4,3,2,1,0:T(8,128)(2,1)S(1)} %stack.15), channel_id=1, replica_groups=mesh['zh'=2,'cx'=4,'tz'=4,'ty'=4,'dp'=2] {'tz','ty'}, dimensions={0} | all-to-all | bytes 16777216 | tf_op jit(solution)/shard_map/all_to_all | solution.py:46
  201.6 1.2 fusion.29
  202.8 0.6 copy.66
  203.3 0.0 copy-start.7
  203.4 0.0 copy-start.10
  203.4 0.6 copy.67
  203.9 0.0 copy-start.2
  204.0 2.5 copy-done.10
  206.4 2.4 fusion.14
  208.8 0.0 copy-done.2
  208.8 0.0 copy-done.7
  208.8 0.0 copy-done.8
  208.8 6.6 %add_convert_fusion = (bf16[2,512,2048]{2,1,0:T(8,128)(2,1)S(1)}, f32[2,2048,512]{1,2,0:T(8,128)}) fusion(bf16[2,512,2048]{2,1,0:T(8,128)(2,1)S(1)} %bitcast.93, bf16[512,512]{1,0:T(8,128)(2,1)S(1)} %copy-done.8), kind=kOutput, calls=%fused_computation.12 | convolution fusion | flops 2170552320 | bytes 17301504 | tf_op jit(solution)/shard_map/tl,blc->btc/dot_general | solution.py:53
  215.4 0.0 copy-done
  215.4 2.3 fusion.11
  217.7 0.4 pad_maximum_fusion
  218.2 0.4 copy.68
  218.6 49.7 %all_to_all.66 = f32[4,256,2,512]{3,1,2,0:T(8,128)} all-to-all(f32[4,256,2,512]{3,1,2,0:T(8,128)S(1)} %copy.68), channel_id=1, replica_groups=mesh['zh'=2,'cx'=4,'tz'=4,'ty'=4,'dp'=2] {'cx'}, dimensions={0} | all-to-all | bytes 8388608 | tf_op jit(solution)/shard_map/all_to_all | solution.py:36
  268.3 2.8 reduce_sum.54
  271.1 0.1 copy.70
  271.2 18.8 %all_to_all.67 = f32[2,128,2,512]{3,1,2,0:T(8,128)S(1)} all-to-all(f32[2,128,2,512]{3,1,2,0:T(8,128)S(1)} %copy.70), channel_id=1, replica_groups=mesh['zh'=2,'cx'=4,'tz'=4,'ty'=4,'dp'=2] {'zh'}, dimensions={0} | all-to-all | bytes 2097152 | tf_op jit(solution)/shard_map/all_to_all | solution.py:36
  290.0 0.9 reduce_sum.55
  290.9 1.2 multiply_convert_fusion
  292.2 16.1 %all_to_all.68 = bf16[2,128,2,512]{3,1,2,0:T(8,128)(2,1)S(1)} all-to-all(bf16[2,128,2,512]{3,1,2,0:T(8,128)(2,1)S(1)} %broadcast_in_dim.40), channel_id=1, replica_groups=mesh['zh'=2,'cx'=4,'tz'=4,'ty'=4,'dp'=2] {'zh'}, dimensions={0} | all-to-all | bytes 1048576 | tf_op jit(solution)/shard_map/all_to_all | solution.py:31
  308.4 0.2 broadcast_in_dim.42
  308.6 18.1 %all_to_all.69 = bf16[4,256,2,512]{3,1,2,0:T(8,128)(2,1)S(1)} all-to-all(bf16[4,256,2,512]{3,1,2,0:T(8,128)(2,1)S(1)} %broadcast_in_dim.42), channel_id=1, replica_groups=mesh['zh'=2,'cx'=4,'tz'=4,'ty'=4,'dp'=2] {'cx'}, dimensions={0} | all-to-all | bytes 4194304 | tf_op jit(solution)/shard_map/all_to_all | solution.py:31
  326.6 0.1 copy.72
  326.8 0.0 copy-start.5
  326.8 0.0 slice-start
  326.8 0.0 slice-start.1
  326.8 2.4 multiply_add_fusion.1
  329.3 0.5 slice-done
  329.7 1.3 slice-done.1
  331.0 5.5 %fusion.6 = bf16[2,512,2048]{2,1,0:T(8,128)(2,1)S(1)} fusion(f32[2,512,2048]{2,1,0:T(8,128)S(1)} %bitcast.82, f32[2,2048,512]{1,2,0:T(8,128)S(1)} %bitcast.89), kind=kLoop, calls=%fused_computation.8 | loop fusion | flops 39845888 | bytes 20971520 | tf_op jit(solution)/shard_map/convert_element_type | solution.py:77
  336.5 1.9 copy-done.4
  338.5 6.0 %bitcast_add_fusion = f32[2,512,2048]{2,1,0:T(8,128)} fusion(f32[2,512,2048]{2,1,0:T(8,128)S(1)} %bitcast.83, bf16[2,512,2048]{2,1,0:T(8,128)(2,1)S(1)} %fusion.6, bf16[512,512]{1,0:T(8,128)(2,1)S(1)} %copy-done.9), kind=kOutput, calls=%fused_computation.9 | convolution fusion | flops 2149580800 | bytes 21495808 | tf_op jit(solution)/shard_map/tl,btc->blc/dot_general | solution.py:78
  344.4 0.0 reduce-scatter.4.cloned.1.call-update
  344.4 0.0 reduce-scatter.6.cloned.1.call-start
  344.5 1.5 copy-done.6
  346.0 6.5 %fusion.18 = f32[2048,512]{1,0:T(8,128)} fusion(bf16[1024,2048]{1,0:T(8,128)(2,1)} %bitcast.105, bf16[1024,2,512]{2,0,1:T(8,128)(2,1)S(1)} %bitcast.91), kind=kOutput, calls=%fused_computation.24 | convolution fusion | flops 2147483648 | bytes 9437184 | tf_op jit(solution)/shard_map/rc,rh->ch/dot_general | solution.py:67
  352.5 0.0 reduce-scatter.6.cloned.1.call-update
  352.5 0.3 reduce-scatter.8.cloned.1.call-start
  352.8 6.5 %fusion.17 = f32[512,2048]{1,0:T(8,128)} fusion(bf16[1024,2048]{1,0:T(8,128)(2,1)} %bitcast.85, bf16[1024,2,512]{2,0,1:T(8,128)(2,1)S(1)} %bitcast.92), kind=kOutput, calls=%fused_computation.22 | convolution fusion | flops 2147483648 | bytes 9437184 | tf_op jit(solution)/shard_map/rh,rc->hc/dot_general | solution.py:68
  359.3 0.0 reduce-scatter.8.cloned.1.call-update
  359.3 5.8 %convolution_bitcast_fusion = f32[2,256,512]{2,1,0:T(8,128)S(1)} fusion(bf16[2,256,2,2048]{3,1,0,2:T(8,128)(2,1)} %bitcast.87, bf16[2,512,2048,1]{2,1,3,0:T(8,128)(2,1)} %bitcast.94), kind=kOutput, calls=%fused_computation.20 | convolution fusion | flops 2147483648 | bytes 9437184 | tf_op jit(solution)/shard_map/btc,blc->tl/dot_general | solution.py:81
  365.2 23.1 %all_to_all.70 = f32[2,256,512]{2,1,0:T(8,128)S(1)} all-to-all(f32[2,256,512]{2,1,0:T(8,128)S(1)} %convolution_bitcast_fusion), channel_id=1, replica_groups=mesh['zh'=2,'cx'=4,'tz'=4,'ty'=4,'dp'=2] {'dp'}, dimensions={0} | all-to-all | bytes 2097152 | tf_op jit(solution)/shard_map/all_to_all | solution.py:36
  388.2 0.1 reduce_sum.56
  388.3 11.4 %all_to_all.71 = f32[4,64,512]{2,1,0:T(8,128)S(1)} all-to-all(f32[4,64,512]{2,1,0:T(8,128)S(1)} %bitcast.99), channel_id=1, replica_groups=mesh['zh'=2,'cx'=4,'tz'=4,'ty'=4,'dp'=2] {'cx'}, dimensions={0} | all-to-all | bytes 1048576 | tf_op jit(solution)/shard_map/all_to_all | solution.py:36
  399.8 11.3 %all_to_all.72 = f32[2,32,512]{2,1,0:T(8,128)S(1)} all-to-all(f32[2,32,512]{2,1,0:T(8,128)S(1)} %bitcast.101), channel_id=1, replica_groups=mesh['zh'=2,'cx'=4,'tz'=4,'ty'=4,'dp'=2] {'zh'}, dimensions={0} | all-to-all | bytes 262144 | tf_op jit(solution)/shard_map/all_to_all | solution.py:36
  411.1 42.9 %all_to_all.73 = f32[16,2,512]{2,1,0:T(2,128)S(1)} all-to-all(f32[16,2,512]{2,1,0:T(2,128)S(1)} %reshape.74), channel_id=1, replica_groups=mesh['zh'=2,'cx'=4,'tz'=4,'ty'=4,'dp'=2] {'tz','ty'}, dimensions={0} | all-to-all | bytes 131072 | tf_op jit(solution)/shard_map/all_to_all | solution.py:36
  454.1 18.8 %all_to_all.74 = f32[16,2,512]{2,1,0:T(2,128)S(1)} all-to-all(f32[16,2,512]{2,1,0:T(2,128)S(1)} %broadcast_in_dim.43), channel_id=1, replica_groups=mesh['zh'=2,'cx'=4,'tz'=4,'ty'=4,'dp'=2] {'tz','ty'}, dimensions={0} | all-to-all | bytes 131072 | tf_op jit(solution)/shard_map/all_to_all | solution.py:31
  472.9 18.1 %all_to_all.75 = f32[2,32,512]{2,1,0:T(8,128)S(1)} all-to-all(f32[2,32,512]{2,1,0:T(8,128)S(1)} %broadcast_in_dim.45), channel_id=1, replica_groups=mesh['zh'=2,'cx'=4,'tz'=4,'ty'=4,'dp'=2] {'zh'}, dimensions={0} | all-to-all | bytes 262144 | tf_op jit(solution)/shard_map/all_to_all | solution.py:31
  491.1 9.6 %all_to_all.76 = f32[4,64,512]{2,1,0:T(8,128)S(1)} all-to-all(f32[4,64,512]{2,1,0:T(8,128)S(1)} %broadcast_in_dim.47), channel_id=1, replica_groups=mesh['zh'=2,'cx'=4,'tz'=4,'ty'=4,'dp'=2] {'cx'}, dimensions={0} | all-to-all | bytes 1048576 | tf_op jit(solution)/shard_map/all_to_all | solution.py:31
  500.7 0.1 broadcast_in_dim.49
  500.9 10.7 %all_to_all.77 = f32[2,256,512]{2,1,0:T(8,128)S(1)} all-to-all(f32[2,256,512]{2,1,0:T(8,128)S(1)} %broadcast_in_dim.49), channel_id=1, replica_groups=mesh['zh'=2,'cx'=4,'tz'=4,'ty'=4,'dp'=2] {'dp'}, dimensions={0} | all-to-all | bytes 2097152 | tf_op jit(solution)/shard_map/all_to_all | solution.py:31
  511.5 1.1 convert_bitcast_fusion
  512.7 1.0 copy.77
  513.7 2.5 reduce-scatter.8.cloned.1.call-done
  516.1 1.0 copy.84
  (26 shorter events, 0.4 us)
Async XLA Ops:
  7.2 208.2 %copy-start = (bf16[2048,512]{1,0:T(8,128)(2,1)S(1)}, bf16[2048,512]{1,0:T(8,128)(2,1)}, u32[]{:S(2)}) copy-start(bf16[2048,512]{1,0:T(8,128)(2,1)} %param.7) | copy-start | bytes 6291460
  7.2 504.4 %reduce-scatter.4.cloned.1.call-start = ((), (), s32[]{:S(2)}) async-start(), calls=%async_computation.16 | async-start | bytes 8912896 | tf_op jit(solution)/shard_map/reduce_scatter | solution.py:79
  203.3 5.4 %copy-start.7 = (bf16[1,2,16,32,2048]{4,3,2,1,0:T(8,128)(2,1)}, bf16[1,2,16,32,2048]{4,3,2,1,0:T(8,128)(2,1)S(1)}, u32[]{:S(2)}) copy-start(bf16[1,2,16,32,2048]{4,3,2,1,0:T(8,128)(2,1)S(1)} %copy.66) | copy-start | bytes 12582916
  203.4 3.1 copy-start.10
  203.9 4.8 copy-start.2
  206.4 2.4 copy-start.8
  215.4 2.3 copy-start.11
  308.5 18.3 %copy-start.3 = (bf16[1,2,16,32,2048]{4,3,2,1,0:T(8,128)(2,1)S(1)}, bf16[1,2,16,32,2048]{4,3,2,1,0:T(8,128)(2,1)}, u32[]{:S(2)}) copy-start(bf16[1,2,16,32,2048]{4,3,2,1,0:T(8,128)(2,1)} %copy-done.2) | copy-start | bytes 12582916
  326.8 2.5 copy-start.5
  326.8 2.9 slice-start
  326.8 4.2 slice-start.1
  331.0 7.4 %copy-start.9 = (bf16[512,512]{1,0:T(8,128)(2,1)S(1)}, bf16[512,512]{1,0:T(8,128)(2,1)}, u32[]{:S(2)}) copy-start(bf16[512,512]{1,0:T(8,128)(2,1)} %param.9) | copy-start | bytes 1572868
  336.5 2.0 copy-start.4
  344.4 1.6 copy-start.6
  344.4 169.2 %reduce-scatter.6.cloned.1.call-start = ((), (), s32[]{:S(2)}) async-start(), calls=%async_computation.17 | async-start | bytes 6291456 | tf_op jit(solution)/shard_map/reduce_scatter | solution.py:70
  352.5 163.6 %reduce-scatter.8.cloned.1.call-start = ((), (), s32[]{:S(2)}) async-start(), calls=%async_computation.18 | async-start | bytes 6291456 | tf_op jit(solution)/shard_map/reduce_scatter | solution.py:71
  491.1 26.1 %copy-start.1 = (bf16[2048,512]{1,0:T(8,128)(2,1)S(1)}, bf16[2048,512]{1,0:T(8,128)(2,1)}, u32[]{:S(2)}) copy-start(bf16[2048,512]{1,0:T(8,128)(2,1)} %param.7) | copy-start | bytes 6291460
Sparse Core Ops, SparseCore 0:
  344.6 124.7 reduce-scatter.3
  472.5 21.8 reduce-scatter.5
  497.5 18.6 reduce-scatter.7
